TPU v7x, 32 devices: a whole 2x2x4 slice. The times are simulated.
32 devices in a mesh: row: 8 (over z, y), col: 4 (over x, core).
Axes of the slice: x: 2, y: 2, z: 4, core: 2. Of those that a mesh axis runs over, the one named last changes fastest.
Arguments:
- tokens: bfloat16 [1024, 4096], P('row'), may hold values from -6 to 6
- in_weight: bfloat16 [4096, 8192], P('row', 'col'), may hold values from -0.09375 to 0.09375
- gate_branch: bfloat16 [1024, 8192], P('row', 'col'), may hold values from -6 to 6
- conv_weight: float32 [4, 8192], P(None, 'col'), may hold values from -3 to 3
- out_weight: bfloat16 [8192, 4096], P('col'), may hold values from -0.0625 to 0.0625
- target: bfloat16 [1024, 4096], P('row'), may hold values from -6 to 6
- lang_ids: int32 [1024], P('row'), may hold values from 0 to 31
- lang_weight: float32 [32], replicated, may hold values from 0.25 to 4
- doc_pos: int32 [1024], P('row'), may hold values from 0 to 127, as said below
Outputs:
- block_out: bfloat16 [1024, 4096], P('row', 'col')
- grad_tokens: bfloat16 [1024, 4096], P('row', 'col')
- grad_gate: bfloat16 [1024, 8192], P('row', 'col')
Inputs may be any that keep to these rules, and one draw needn't show every extreme that they name: doc_pos is 0 at the first token and at every document's first token, and otherwise one more than the previous token's; no document is longer than 128 tokens and one is exactly 128 tokens long; apart from token 0, no document begins within the first 4 tokens of an aligned block of 128 tokens.
All inputs are finite; a program needn't handle non-finite values.
Results may differ from a plain program's by a relative error of at most 0.022.
Values may be sent and summed in bfloat16 or wider, within the bound.
No kernel may reach another device: no remote copies, remote signals or barrier semaphores. Data moves between devices by JAX's collectives and lax.ppermute only.
A program may use at most 128 MiB of HBM per device.

v0:
```python
import jax
import jax.numpy as jnp
from jax import lax
from jax.sharding import PartitionSpec as P

CONV = 4
LANGS = 32


def passed_along(value, axis, steps):
    count = lax.axis_size(axis)
    first, last = (max(0, -steps), min(count, count - steps))
    return lax.ppermute(value, axis, [(source, source + steps) for source in range(first, last)])


def silu_grad(argument):
    sigmoid_v = jax.nn.sigmoid(argument)
    return sigmoid_v * (1.0 + argument * (1.0 - sigmoid_v))


def shards(
    tokens, in_weight, gate_branch, conv_weight, out_weight, target, lang_ids, lang_weight, doc_pos
):
    row_count = tokens.shape[0]
    inner_width = gate_branch.shape[1]
    margin = CONV - 1
    moves_tokens = row_count * lax.axis_size("row") < tokens.shape[1]
    if moves_tokens:
        token_cols = lax.all_to_all(tokens, "row", 1, 0, tiled=True)
        part_x = jnp.dot(token_cols, in_weight, preferred_element_type=jnp.float32)
        inner_x = lax.psum_scatter(
            part_x.astype(jnp.bfloat16), "row", scatter_dimension=0, tiled=True
        )
    else:
        full_in = lax.all_gather(in_weight, "row", axis=0, tiled=True)
        inner_x = jnp.dot(tokens, full_in, preferred_element_type=jnp.float32).astype(jnp.bfloat16)
    from_prev = passed_along(inner_x[row_count - margin :], "row", 1)
    extended = jnp.concatenate([from_prev, inner_x], axis=0).astype(jnp.float32)
    conv_sum = jnp.zeros((row_count, inner_width), jnp.float32)
    for offset in range(CONV):
        keep_mask = (doc_pos >= offset).astype(jnp.float32)[:, None]
        conv_sum = (
            conv_sum
            + conv_weight[offset][None, :]
            * extended[margin - offset : margin - offset + row_count]
            * keep_mask
        )
    gate_value = gate_branch.astype(jnp.float32)
    gate_act = jax.nn.silu(gate_value)
    conv_act = jax.nn.silu(conv_sum)
    mixed = (conv_act * gate_act).astype(jnp.bfloat16)
    partial_value = jnp.dot(mixed, out_weight, preferred_element_type=jnp.float32)
    columns = tokens.shape[1] // lax.axis_size("col")
    col_start = lax.axis_index("col") * columns
    lang_table = (lang_ids[:, None] == jnp.arange(LANGS, dtype=jnp.int32)[None, :]).astype(
        jnp.float32
    )
    token_weight = jnp.sum(lang_table * lang_weight[None, :], axis=1)[:, None]
    out_total = lax.psum(partial_value.astype(jnp.bfloat16), "col").astype(jnp.float32)
    out_block = lax.dynamic_slice_in_dim(out_total, col_start, columns, 1)
    residual_grad = (token_weight * (out_total - target.astype(jnp.float32))).astype(jnp.bfloat16)
    grad_mixed = lax.dot_general(
        residual_grad, out_weight, (((1,), (1,)), ((), ())), preferred_element_type=jnp.float32
    )
    grad_conv = grad_mixed * gate_act * silu_grad(conv_sum)
    grad_gate = (grad_mixed * conv_act * silu_grad(gate_value)).astype(jnp.bfloat16)
    local_grad = conv_weight[0][None, :] * grad_conv
    spill_over = jnp.zeros((margin, inner_width), jnp.float32)
    for offset in range(1, CONV):
        masked = (
            conv_weight[offset][None, :]
            * grad_conv
            * (doc_pos >= offset).astype(jnp.float32)[:, None]
        )
        local_grad = local_grad + jnp.concatenate(
            [masked[offset:], jnp.zeros((offset, inner_width), jnp.float32)], axis=0
        )
        spill_over = spill_over + jnp.concatenate(
            [jnp.zeros((margin - offset, inner_width), jnp.float32), masked[:offset]], axis=0
        )
    from_next = passed_along(spill_over, "row", -1)
    grad_x = (
        local_grad
        + jnp.concatenate(
            [jnp.zeros((row_count - margin, inner_width), jnp.float32), from_next], axis=0
        )
    ).astype(jnp.bfloat16)
    if moves_tokens:
        grad_x_all = lax.all_gather(grad_x, "row", axis=0, tiled=True)
        grad_cols = lax.dot_general(
            grad_x_all, in_weight, (((1,), (1,)), ((), ())), preferred_element_type=jnp.float32
        )
        partial_grad = lax.all_to_all(grad_cols.astype(jnp.bfloat16), "row", 0, 1, tiled=True)
    else:
        partial_grad = lax.dot_general(
            grad_x, full_in, (((1,), (1,)), ((), ())), preferred_element_type=jnp.float32
        )
    grad_tokens = lax.psum_scatter(
        partial_grad.astype(jnp.bfloat16), "col", scatter_dimension=1, tiled=True
    )
    return (out_block.astype(jnp.bfloat16), grad_tokens, grad_gate)


def solution(mesh):
    in_specs = (
        P("row", None),
        P("row", "col"),
        P("row", "col"),
        P(None, "col"),
        P("col", None),
        P("row", None),
        P("row"),
        P(),
        P("row"),
    )
    out_specs = (P("row", "col"), P("row", "col"), P("row", "col"))
    return jax.shard_map(shards, mesh=mesh, in_specs=in_specs, out_specs=out_specs, check_vma=False)
```

profile of v0, /device:TPU:0, one launch (start us, length us, event | category | flops | bytes accessed | tf_op | source)
XLA Modules:
  0.0 352.7 jit_solution(13760163877622993587)
XLA Ops:
  7.2 2.4 copy.17
  9.6 33.0 %all_to_all.38 = bf16[128,8,512]{0,2,1:T(8,128)(2,1)S(1)} all-to-all(bf16[128,8,512]{0,2,1:T(8,128)(2,1)} %bitcast.20), channel_id=1, replica_groups=mesh['row'=8,'col'=4] {'row'}, dimensions={1} | all-to-all | bytes 2097152 | tf_op jit(solution)/shard_map/all_to_all | solution.py:29
  42.7 1.3 copy.18
  44.0 5.5 %convolution_convert_fusion.1 = bf16[1024,2048]{1,0:T(8,128)(2,1)} fusion(bf16[1024,512]{1,0:T(8,128)(2,1)} %bitcast.21, bf16[512,2048]{1,0:T(8,128)(2,1)S(1)} %copy-done), kind=kOutput, calls=%fused_computation.1 | convolution fusion | flops 2149580800 | bytes 7340032 | tf_op jit(solution)/shard_map/dot_general | solution.py:30
  49.5 0.0 all-reduce.8.cloned.1.call-start
  49.6 0.7 copy-done.3
  50.3 86.5 %reduce-scatter.3.cloned.1.call-done = bf16[128,2048]{1,0:T(8,128)(2,1)} async-done(((bf16[1024,2048]{1,0:T(8,128)(2,1)}), bf16[128,2048]{1,0:T(8,128)(2,1)}) %reduce-scatter.3.cloned.1.call-update) | async-done | bytes 524304 | tf_op jit(solution)/shard_map/reduce_scatter | solution.py:31
  136.8 0.8 slice.64
  137.6 3.4 collective-permute-start
  141.0 1.4 collective-permute-done
  142.4 1.2 maximum_convert_fusion
  143.6 0.7 fusion.9
  144.3 1.0 copy-done.2
  145.3 9.5 %convolution_convert_fusion = bf16[128,4096]{1,0:T(8,128)(2,1)} fusion(bf16[2048,4096]{1,0:T(8,128)(2,1)} %param.13, bf16[128,2048]{1,0:T(8,128)(2,1)S(1)} %copy-done.5, f32[128,2048]{1,0:T(8,128)S(1)} %fusion.9), kind=kOutput, calls=%fused_computation | convolution fusion | flops 2150891520 | bytes 19398656 | tf_op jit(solution)/shard_map/dot_general | solution.py:52
  154.9 0.1 select_reduce_fusion
  154.9 36.6 %all-reduce.8.cloned.1.call-done = bf16[128,4096]{1,0:T(8,128)(2,1)} async-done(((bf16[128,4096]{1,0:T(8,128)(2,1)}), bf16[128,4096]{1,0:T(8,128)(2,1)}) %all-reduce.8.cloned.1.call-update) | async-done | bytes 1048592 | tf_op jit(solution)/shard_map/psum | solution.py:59
  191.6 14.1 %multiply_multiply_fusion.2 = (f32[128,2048]{1,0:T(8,128)}, f32[128,2048]{1,0:T(8,128)S(1)}, bf16[128,2048]{1,0:T(8,128)(2,1)}) fusion(f32[128]{0:T(128)S(1)} %get-tuple-element.13, f32[2048]{0:T(1024)S(1)} %bitcast.30, f32[128,2048]{1,0:T(8,128)} %copy-done.2, bf16[128,2048]{1,0:T(8,128)(2,1)} %param.11, bf16[2048,4096]{1,0:T(8,128)(2,1)} %param.13, ...), kind=kOutput, calls=%fused_computation.29 | convolution fusion | flops 2156396544 | bytes 23077888 | tf_op jit(solution)/shard_map/dot_general | solution.py:62
  205.7 0.9 slice.72
  206.6 0.3 multiply_multiply_fusion.1
  206.9 1.5 collective-permute-start.1
  208.4 0.1 slice.69
  208.5 0.1 slice.70
  208.6 0.1 slice.71
  208.7 4.0 %collective-permute-done.1 = f32[3,2048]{1,0:T(4,128)S(1)} collective-permute-done((f32[3,2048]{1,0:T(4,128)S(1)}, f32[3,2048]{1,0:T(4,128)S(1)}, u32[]{:S(2)}, u32[]{:S(2)}) %collective-permute-start.1) | collective-permute-done | bytes 24608 | tf_op jit(solution)/shard_map/ppermute | solution.py:13
  212.7 1.2 add_convert_fusion
  213.9 0.0 reduce-scatter.5.cloned.1.call-start
  214.0 73.9 %all-gather.2.cloned.1.call-done = bf16[1024,2048]{1,0:T(8,128)(2,1)} async-done(((bf16[128,2048]{1,0:T(8,128)(2,1)}), bf16[1024,2048]{1,0:T(8,128)(2,1)}) %all-gather.2.cloned.1.call-update) | async-done | bytes 4194320 | tf_op jit(solution)/shard_map/all_gather | solution.py:89
  287.9 4.5 %convolution_convert_fusion.2 = bf16[1024,512]{1,0:T(8,128)(2,1)S(1)} fusion(bf16[1024,2048]{1,0:T(8,128)(2,1)} %all-gather.2.cloned.1.call-done, bf16[512,2048]{1,0:T(8,128)(2,1)S(1)} %copy-done), kind=kOutput, calls=%fused_computation.6 | convolution fusion | flops 2148007936 | bytes 7340032 | tf_op jit(solution)/shard_map/dot_general | solution.py:90
  292.4 28.5 %all_to_all.39 = bf16[8,128,512]{2,1,0:T(8,128)(2,1)S(1)} all-to-all(bf16[8,128,512]{2,1,0:T(8,128)(2,1)S(1)} %bitcast.22), channel_id=1, replica_groups=mesh['row'=8,'col'=4] {'row'}, dimensions={0} | all-to-all | bytes 2097152 | tf_op jit(solution)/shard_map/all_to_all | solution.py:93
  321.0 1.1 copy.20
  322.1 1.7 dynamic-slice_convert_fusion
  323.8 22.4 %reduce-scatter.5.cloned.1.call-done = bf16[128,1024]{1,0:T(8,128)(2,1)} async-done(((bf16[128,4096]{1,0:T(8,128)(2,1)}), bf16[128,1024]{1,0:T(8,128)(2,1)}) %reduce-scatter.5.cloned.1.call-update) | async-done | bytes 262160 | tf_op jit(solution)/shard_map/reduce_scatter | solution.py:98
  (24 shorter events, 0.2 us)
Async XLA Ops:
  7.2 36.8 %copy-start = (bf16[512,2048]{1,0:T(8,128)(2,1)S(1)}, bf16[512,2048]{1,0:T(8,128)(2,1)}, u32[]{:S(2)}) copy-start(bf16[512,2048]{1,0:T(8,128)(2,1)} %param.10) | copy-start | bytes 6291460
  7.2 129.6 %reduce-scatter.3.cloned.1.call-start = ((), (), s32[]{:S(2)}) async-start(), calls=%async_computation.4 | async-start | bytes 4718592 | tf_op jit(solution)/shard_map/reduce_scatter | solution.py:31
  49.5 0.8 copy-start.3
  49.5 91.4 %copy-start.4 = (s32[128]{0:T(128)S(1)}, s32[128]{0:T(128)}, u32[]{:S(2)}) copy-start(s32[128]{0:T(128)} %param.17) | copy-start | bytes 1540
  49.5 142.1 %all-reduce.8.cloned.1.call-start = ((), (), s32[]{:S(2)}) async-start(), calls=%async_computation.5 | async-start | bytes 2097152 | tf_op jit(solution)/shard_map/psum | solution.py:59
  137.6 4.8 %collective-permute-start = (bf16[3,2048]{1,0:T(4,128)(2,1)S(1)}, bf16[3,2048]{1,0:T(4,128)(2,1)S(1)}, u32[]{:S(2)}, u32[]{:S(2)}) collective-permute-start(bf16[3,2048]{1,0:T(4,128)(2,1)S(1)} %slice.64), channel_id=1, source_target_pairs={{0,4},{4,8},{8,12},{12,16},{16,20},{20,24},{24,28},{1,5},{5,9},{9,... | collective-permute-start | bytes 36872 | tf_op jit(solution)/shard_map/ppermute | solution.py:13
  143.6 1.7 copy-start.5
  144.3 1.0 copy-start.2
  145.3 9.5 %copy-start.6 = (f32[32]{0:T(128)S(1)}, f32[32]{0:T(128)}, u32[]{:S(2)}) copy-start(f32[32]{0:T(128)} %param.16) | copy-start | bytes 388
  145.3 9.5 %copy-start.7 = (s32[128]{0:T(128)S(1)}, s32[128]{0:T(128)}, u32[]{:S(2)}) copy-start(s32[128]{0:T(128)} %param.15) | copy-start | bytes 1540
  154.8 133.1 %all-gather.2.cloned.1.call-start = ((), (), s32[]{:S(2)}) async-start(), calls=%async_computation.6 | async-start | bytes 4718592 | tf_op jit(solution)/shard_map/all_gather | solution.py:89
  205.7 2.7 copy-start.1
  206.9 5.8 %collective-permute-start.1 = (f32[3,2048]{1,0:T(4,128)S(1)}, f32[3,2048]{1,0:T(4,128)S(1)}, u32[]{:S(2)}, u32[]{:S(2)}) collective-permute-start(f32[3,2048]{1,0:T(4,128)S(1)} %slice_add_fusion), channel_id=1, source_target_pairs={{4,0},{8,4},{12,8},{16,12},{20,16},{24,20},{28,24},{5,1},{9,5},{13... | collective-permute-start | bytes 73736 | tf_op jit(solution)/shard_map/ppermute | solution.py:13
  213.9 132.2 %reduce-scatter.5.cloned.1.call-start = ((), (), s32[]{:S(2)}) async-start(), calls=%async_computation.7 | async-start | bytes 1310720 | tf_op jit(solution)/shard_map/reduce_scatter | solution.py:98
Sparse Core Ops, SparseCore 0:
  49.7 87.0 reduce-scatter.2
  154.9 36.6 all-reduce.7
  214.1 73.7 all-gather.1
  322.2 23.9 reduce-scatter.4
where the time goes:
time: 353 us
  waiting for transfers between devices  225 us (64%)
  blocking collectives  61.6 us (17%)
  matrix products  33.6 us (10%)
  between operations  13.9 us (4%)
  local copies, waits for them, and re-layouts  10.2 us (3%)
  starting transfers between devices  5.03 us (1%)
    reduce_scatter x1, waiting for transfers between devices, shards(): lax.psum_scatter(part_x.astype(jnp.bfloat16), 'row', scatter_dimension=0,...  86.5 us
    all_gather x1, waiting for transfers between devices, shards(): grad_x_all = lax.all_gather(grad_x, 'row', axis=0, tiled=True)  73.9 us
    psum x1, waiting for transfers between devices, shards(): lax.psum(partial_value.astype(jnp.bfloat16), 'col').astype(jnp.float32)  36.6 us
    all_to_all x1, blocking collectives, shards(): token_cols = lax.all_to_all(tokens, 'row', 1, 0, tiled=True)  33 us
    all_to_all x1, blocking collectives, shards(): lax.all_to_all(grad_cols.astype(jnp.bfloat16), 'row', 0, 1, tiled=True)  28.5 us
    reduce_scatter x1, waiting for transfers between devices, shards(): lax.psum_scatter(partial_grad.astype(jnp.bfloat16), 'col', scatter_dimens...  22.4 us
    dot_general x1, matrix products, shards(): lax.dot_general(residual_grad, out_weight, (((1,), (1,)), ((), ())), pref...  14.1 us
    dot_general x1, matrix products, shards(): jnp.dot(mixed, out_weight, preferred_element_type=jnp.float32)  9.46 us
  transfers between devices with their start and end apart: 6, of which 6 were waited for; matrix products, arithmetic and copies ran while one was open for 1% of the time, Pallas kernels for 0%

commit v1 on v0

--- a/solution.py
+++ b/solution.py
@@ -1,3 +1,4 @@
+import functools
 import jax
 import jax.numpy as jnp
 from jax import lax
@@ -5,6 +6,21 @@
 
 CONV = 4
 LANGS = 32
+
+
+def store_seats_all_now(buf, axis_key, array_axis):
+    amount_of = lax.axis_size(axis_key)
+    arrivals = list(map(lambda w: (w, (w + 1) % amount_of), range(amount_of)))
+    z = [None] * amount_of
+    z[amount_of - 1] = buf
+    for i0 in range(amount_of - 2, -1, -1):
+        z[i0] = lax.ppermute(z[i0 + 1], axis_name=axis_key, perm=arrivals)
+    passed = jnp.concatenate(z, array_axis)
+    out_arr = jnp.roll(passed, (lax.axis_index(axis_key) + 1) * buf.shape[array_axis], array_axis)
+    return out_arr
+
+
+_arrange_grid = functools.partial(store_seats_all_now, axis_key="row", array_axis=0)
 
 
 def passed_along(value, axis, steps):
@@ -86,7 +102,7 @@
         )
     ).astype(jnp.bfloat16)
     if moves_tokens:
-        grad_x_all = lax.all_gather(grad_x, "row", axis=0, tiled=True)
+        grad_x_all = _arrange_grid(grad_x)
         grad_cols = lax.dot_general(
             grad_x_all, in_weight, (((1,), (1,)), ((), ())), preferred_element_type=jnp.float32
         )

time: 353 us -> 374 us (1.059)
  waiting for transfers between devices: 225 us -> 240 us
  local copies, waits for them, and re-layouts: 10.2 us -> 22.8 us
  blocking collectives: 61.6 us -> 53.1 us
    ppermute x0 -> x7, waiting for transfers between devices: none -> 90.1 us  [store_seats_all_now(): z[i0] = lax.ppermute(z[i0 + 1], axis_name=axis_key, perm=arrivals)]
    all_gather x1 -> x0, waiting for transfers between devices: 73.9 us -> none  [shards(): grad_x_all = lax.all_gather(grad_x, 'row', axis=0, tiled=True)]
    unnamed x17 -> x48, local copies, waits for them, and re-layouts: 4.1 us -> 15.5 us
    all_to_all x1, blocking collectives: 28.5 us -> 20.1 us  [shards(): lax.all_to_all(grad_cols.astype(jnp.bfloat16), 'row', 0, 1, tiled=True)]
  transfers between devices with their start and end apart: 6 -> 12, of which waited for: 6 -> 12; matrix products, arithmetic and copies ran while one was open for 1% -> 1% of each run, Pallas kernels for 0% -> 0%
where the time goes in v1:
time: 374 us; the launch traced here: 373 us
  waiting for transfers between devices  240 us (64%)
  blocking collectives  53.1 us (14%)
  matrix products  31.4 us (8%)
  local copies, waits for them, and re-layouts  22.8 us (6%)
  between operations  14.1 us (4%)
  starting transfers between devices  7.4 us (2%)
  other arithmetic  3.87 us (1%)
    ppermute x7, waiting for transfers between devices, store_seats_all_now(): z[i0] = lax.ppermute(z[i0 + 1], axis_name=axis_key, perm=arrivals)  90.1 us
    reduce_scatter x1, waiting for transfers between devices, shards(): lax.psum_scatter(part_x.astype(jnp.bfloat16), 'row', scatter_dimension=0,...  87 us
    psum x1, waiting for transfers between devices, shards(): lax.psum(partial_value.astype(jnp.bfloat16), 'col').astype(jnp.float32)  36.6 us
    all_to_all x1, blocking collectives, shards(): token_cols = lax.all_to_all(tokens, 'row', 1, 0, tiled=True)  33 us
    reduce_scatter x1, waiting for transfers between devices, shards(): lax.psum_scatter(partial_grad.astype(jnp.bfloat16), 'col', scatter_dimens...  22.1 us
    all_to_all x1, blocking collectives, shards(): lax.all_to_all(grad_cols.astype(jnp.bfloat16), 'row', 0, 1, tiled=True)  20.1 us
    unnamed x48, local copies, waits for them, and re-layouts  15.5 us
    dot_general x1, matrix products, shards(): lax.dot_general(residual_grad, out_weight, (((1,), (1,)), ((), ())), pref...  14.1 us
  transfers between devices with their start and end apart: 12, of which 12 were waited for; matrix products, arithmetic and copies ran while one was open for 1% of the time, Pallas kernels for 0%

profile of v1, /device:TPU:0, one launch (start us, length us, event | category | flops | bytes accessed | tf_op | source)
XLA Modules:
  0.0 372.7 jit_solution(6157833853131735647)
XLA Ops:
  7.2 2.4 copy.17
  9.6 33.0 %all_to_all.38 = bf16[128,8,512]{0,2,1:T(8,128)(2,1)S(1)} all-to-all(bf16[128,8,512]{0,2,1:T(8,128)(2,1)} %bitcast.19), channel_id=1, replica_groups=mesh['row'=8,'col'=4] {'row'}, dimensions={1} | all-to-all | bytes 2097152 | tf_op jit(solution)/shard_map/all_to_all | solution.py:45
  42.7 1.3 copy.18
  44.0 5.5 %convolution_convert_fusion.1 = bf16[1024,2048]{1,0:T(8,128)(2,1)} fusion(bf16[1024,512]{1,0:T(8,128)(2,1)} %bitcast.21, bf16[512,2048]{1,0:T(8,128)(2,1)S(1)} %copy-done), kind=kOutput, calls=%fused_computation.3 | convolution fusion | flops 2149580800 | bytes 7340032 | tf_op jit(solution)/shard_map/dot_general | solution.py:46
  49.7 87.0 %reduce-scatter.3.cloned.1.call-done = bf16[128,2048]{1,0:T(8,128)(2,1)} async-done(((bf16[1024,2048]{1,0:T(8,128)(2,1)}), bf16[128,2048]{1,0:T(8,128)(2,1)}) %reduce-scatter.3.cloned.1.call-update) | async-done | bytes 524304 | tf_op jit(solution)/shard_map/reduce_scatter | solution.py:47
  137.4 3.4 collective-permute-start
  140.8 1.4 collective-permute-done
  142.2 1.2 maximum_convert_fusion
  145.1 9.4 %convolution_convert_fusion = bf16[128,4096]{1,0:T(8,128)(2,1)} fusion(bf16[2048,4096]{1,0:T(8,128)(2,1)} %param.13, bf16[128,2048]{1,0:T(8,128)(2,1)S(1)} %copy-done.13, f32[128,2048]{1,0:T(8,128)S(1)} %fusion.14), kind=kOutput, calls=%fused_computation | convolution fusion | flops 2150891520 | bytes 19398656 | tf_op jit(solution)/shard_map/dot_general | solution.py:68
  154.7 36.6 %all-reduce.8.cloned.1.call-done = bf16[128,4096]{1,0:T(8,128)(2,1)} async-done(((bf16[128,4096]{1,0:T(8,128)(2,1)}), bf16[128,4096]{1,0:T(8,128)(2,1)}) %all-reduce.8.cloned.1.call-update) | async-done | bytes 1048592 | tf_op jit(solution)/shard_map/psum | solution.py:75
  191.4 14.1 %multiply_multiply_fusion.2 = (f32[128,2048]{1,0:T(8,128)}, f32[128,2048]{1,0:T(8,128)S(1)}, bf16[128,2048]{1,0:T(8,128)(2,1)}) fusion(f32[128]{0:T(128)S(1)} %get-tuple-element.13, f32[2048]{0:T(1024)S(1)} %bitcast.29, f32[128,2048]{1,0:T(8,128)} %copy-done.10, bf16[128,2048]{1,0:T(8,128)(2,1)} %param.11, bf16[2048,4096]{1,0:T(8,128)(2,1)} %param.13, ...), kind=kOutput, calls=%fused_computation.31 | convolution fusion | flops 2156396544 | bytes 23077888 | tf_op jit(solution)/shard_map/dot_general | solution.py:78
  206.7 1.5 collective-permute-start.1
  208.1 1.3 slice.69
  209.6 2.8 collective-permute-done.1
  212.5 1.6 add_convert_fusion
  214.0 2.4 collective-permute-start.2
  216.5 12.6 %collective-permute-done.2 = bf16[128,2048]{1,0:T(8,128)(2,1)S(1)} collective-permute-done((bf16[128,2048]{1,0:T(8,128)(2,1)S(1)}, bf16[128,2048]{1,0:T(8,128)(2,1)S(1)}, u32[]{:S(2)}, u32[]{:S(2)}) %collective-permute-start.2) | collective-permute-done | bytes 524320 | tf_op jit(solution)/shard_map/ppermute | solution.py:17
  229.1 14.1 %collective-permute-done.3 = bf16[128,2048]{1,0:T(8,128)(2,1)S(1)} collective-permute-done((bf16[128,2048]{1,0:T(8,128)(2,1)S(1)}, bf16[128,2048]{1,0:T(8,128)(2,1)S(1)}, u32[]{:S(2)}, u32[]{:S(2)}) %collective-permute-start.3) | collective-permute-done | bytes 524320 | tf_op jit(solution)/shard_map/ppermute | solution.py:17
  244.0 13.1 %collective-permute-done.4 = bf16[128,2048]{1,0:T(8,128)(2,1)S(1)} collective-permute-done((bf16[128,2048]{1,0:T(8,128)(2,1)S(1)}, bf16[128,2048]{1,0:T(8,128)(2,1)S(1)}, u32[]{:S(2)}, u32[]{:S(2)}) %collective-permute-start.4) | collective-permute-done | bytes 524320 | tf_op jit(solution)/shard_map/ppermute | solution.py:17
  257.9 12.2 %collective-permute-done.5 = bf16[128,2048]{1,0:T(8,128)(2,1)S(1)} collective-permute-done((bf16[128,2048]{1,0:T(8,128)(2,1)S(1)}, bf16[128,2048]{1,0:T(8,128)(2,1)S(1)}, u32[]{:S(2)}, u32[]{:S(2)}) %collective-permute-start.5) | collective-permute-done | bytes 524320 | tf_op jit(solution)/shard_map/ppermute | solution.py:17
  270.9 12.1 %collective-permute-done.6 = bf16[128,2048]{1,0:T(8,128)(2,1)S(1)} collective-permute-done((bf16[128,2048]{1,0:T(8,128)(2,1)S(1)}, bf16[128,2048]{1,0:T(8,128)(2,1)S(1)}, u32[]{:S(2)}, u32[]{:S(2)}) %collective-permute-start.6) | collective-permute-done | bytes 524320 | tf_op jit(solution)/shard_map/ppermute | solution.py:17
  283.8 13.8 %collective-permute-done.7 = bf16[128,2048]{1,0:T(8,128)(2,1)} collective-permute-done((bf16[128,2048]{1,0:T(8,128)(2,1)S(1)}, bf16[128,2048]{1,0:T(8,128)(2,1)}, u32[]{:S(2)}, u32[]{:S(2)}) %collective-permute-start.7) | collective-permute-done | bytes 524320 | tf_op jit(solution)/shard_map/ppermute | solution.py:17
  297.6 12.2 %collective-permute-done.8 = bf16[128,2048]{1,0:T(8,128)(2,1)} collective-permute-done((bf16[128,2048]{1,0:T(8,128)(2,1)}, bf16[128,2048]{1,0:T(8,128)(2,1)}, u32[]{:S(2)}, u32[]{:S(2)}) %collective-permute-start.8) | collective-permute-done | bytes 524320 | tf_op jit(solution)/shard_map/ppermute | solution.py:17
  310.9 1.1 constant_dynamic-update-slice_fusion.14
  312.0 1.1 constant_dynamic-update-slice_fusion.13
  313.1 1.1 constant_dynamic-update-slice_fusion.12
  316.4 1.1 constant_dynamic-update-slice_fusion.7
  317.5 1.1 constant_dynamic-update-slice_fusion.6
  318.9 2.4 fusion.2
  321.3 20.1 %all_to_all.39 = bf16[8,128,512]{2,1,0:T(8,128)(2,1)S(1)} all-to-all(bf16[8,128,512]{2,1,0:T(8,128)(2,1)S(1)} %bitcast.20), channel_id=1, replica_groups=mesh['row'=8,'col'=4] {'row'}, dimensions={0} | all-to-all | bytes 2097152 | tf_op jit(solution)/shard_map/all_to_all | solution.py:109
  342.5 1.7 dynamic-slice_convert_fusion
  344.1 22.1 %reduce-scatter.5.cloned.1.call-done = bf16[128,1024]{1,0:T(8,128)(2,1)} async-done(((bf16[128,4096]{1,0:T(8,128)(2,1)}), bf16[128,1024]{1,0:T(8,128)(2,1)}) %reduce-scatter.5.cloned.1.call-update) | async-done | bytes 262160 | tf_op jit(solution)/shard_map/reduce_scatter | solution.py:114
  (67 shorter events, 12.0 us)
Async XLA Ops:
  7.2 36.8 %copy-start = (bf16[512,2048]{1,0:T(8,128)(2,1)S(1)}, bf16[512,2048]{1,0:T(8,128)(2,1)}, u32[]{:S(2)}) copy-start(bf16[512,2048]{1,0:T(8,128)(2,1)} %param.10) | copy-start | bytes 6291460
  7.2 129.5 %reduce-scatter.3.cloned.1.call-start = ((), (), s32[]{:S(2)}) async-start(), calls=%async_computation.4 | async-start | bytes 4718592 | tf_op jit(solution)/shard_map/reduce_scatter | solution.py:47
  44.0 5.6 %copy-start.11 = (f32[4,2048]{1,0:T(4,128)S(1)}, f32[4,2048]{1,0:T(4,128)}, u32[]{:S(2)}) copy-start(f32[4,2048]{1,0:T(4,128)} %param.12) | copy-start | bytes 98308
  44.0 96.8 %copy-start.12 = (s32[128]{0:T(128)S(1)}, s32[128]{0:T(128)}, u32[]{:S(2)}) copy-start(s32[128]{0:T(128)} %param.17) | copy-start | bytes 1540
  49.5 95.6 %copy-start.13 = (bf16[128,2048]{1,0:T(8,128)(2,1)S(1)}, bf16[128,2048]{1,0:T(8,128)(2,1)}, u32[]{:S(2)}) copy-start(bf16[128,2048]{1,0:T(8,128)(2,1)} %param.11) | copy-start | bytes 1572868
  49.6 141.8 %all-reduce.8.cloned.1.call-start = ((), (), s32[]{:S(2)}) async-start(), calls=%async_computation.5 | async-start | bytes 2097152 | tf_op jit(solution)/shard_map/psum | solution.py:75
  137.4 4.8 %collective-permute-start = (bf16[3,2048]{1,0:T(4,128)(2,1)S(1)}, bf16[3,2048]{1,0:T(4,128)(2,1)S(1)}, u32[]{:S(2)}, u32[]{:S(2)}) collective-permute-start(bf16[3,2048]{1,0:T(4,128)(2,1)S(1)} %slice.64), channel_id=1, source_target_pairs={{0,4},{4,8},{8,12},{12,16},{16,20},{20,24},{24,28},{1,5},{5,9},{9,... | collective-permute-start | bytes 36872 | tf_op jit(solution)/shard_map/ppermute | solution.py:29
  144.1 1.0 copy-start.10
  145.1 9.5 %copy-start.14 = (f32[32]{0:T(128)S(1)}, f32[32]{0:T(128)}, u32[]{:S(2)}) copy-start(f32[32]{0:T(128)} %param.16) | copy-start | bytes 388
  145.1 9.5 %copy-start.15 = (s32[128]{0:T(128)S(1)}, s32[128]{0:T(128)}, u32[]{:S(2)}) copy-start(s32[128]{0:T(128)} %param.15) | copy-start | bytes 1540
  154.6 211.6 %reduce-scatter.5.cloned.1.call-start = ((), (), s32[]{:S(2)}) async-start(), calls=%async_computation.6 | async-start | bytes 1310720 | tf_op jit(solution)/shard_map/reduce_scatter | solution.py:114
  205.4 4.2 %copy-start.1 = (f32[128,2048]{1,0:T(8,128)}, f32[128,2048]{1,0:T(8,128)S(1)}, u32[]{:S(2)}) copy-start(f32[128,2048]{1,0:T(8,128)S(1)} %get-tuple-element.4) | copy-start | bytes 3145732
  206.7 5.8 %collective-permute-start.1 = (f32[3,2048]{1,0:T(4,128)S(1)}, f32[3,2048]{1,0:T(4,128)S(1)}, u32[]{:S(2)}, u32[]{:S(2)}) collective-permute-start(f32[3,2048]{1,0:T(4,128)S(1)} %slice_add_fusion), channel_id=1, source_target_pairs={{4,0},{8,4},{12,8},{16,12},{20,16},{24,20},{28,24},{5,1},{9,5},{13... | collective-permute-start | bytes 73736 | tf_op jit(solution)/shard_map/ppermute | solution.py:29
  214.0 15.0 %collective-permute-start.2 = (bf16[128,2048]{1,0:T(8,128)(2,1)S(1)}, bf16[128,2048]{1,0:T(8,128)(2,1)S(1)}, u32[]{:S(2)}, u32[]{:S(2)}) collective-permute-start(bf16[128,2048]{1,0:T(8,128)(2,1)S(1)} %add_convert_fusion), channel_id=1, source_target_pairs={{0,4},{4,8},{8,12},{12,16},{16,20},{20,24},{24,28},{28,0},{1,5},{5... | collective-permute-start | bytes 1572872 | tf_op jit(solution)/shard_map/ppermute | solution.py:17
  229.1 14.1 %collective-permute-start.3 = (bf16[128,2048]{1,0:T(8,128)(2,1)S(1)}, bf16[128,2048]{1,0:T(8,128)(2,1)S(1)}, u32[]{:S(2)}, u32[]{:S(2)}) collective-permute-start(bf16[128,2048]{1,0:T(8,128)(2,1)S(1)} %collective-permute-done.2), channel_id=1, source_target_pairs={{0,4},{4,8},{8,12},{12,16},{16,20},{20,24},{24,28},{28,0},{1,5},{5... | collective-permute-start | bytes 1572872 | tf_op jit(solution)/shard_map/ppermute | solution.py:17
  243.1 0.8 copy-start.2
  244.0 13.1 %collective-permute-start.4 = (bf16[128,2048]{1,0:T(8,128)(2,1)S(1)}, bf16[128,2048]{1,0:T(8,128)(2,1)S(1)}, u32[]{:S(2)}, u32[]{:S(2)}) collective-permute-start(bf16[128,2048]{1,0:T(8,128)(2,1)S(1)} %collective-permute-done.3), channel_id=1, source_target_pairs={{0,4},{4,8},{8,12},{12,16},{16,20},{20,24},{24,28},{28,0},{1,5},{5... | collective-permute-start | bytes 1572872 | tf_op jit(solution)/shard_map/ppermute | solution.py:17
  257.1 0.8 copy-start.4
  257.9 12.2 %collective-permute-start.5 = (bf16[128,2048]{1,0:T(8,128)(2,1)S(1)}, bf16[128,2048]{1,0:T(8,128)(2,1)S(1)}, u32[]{:S(2)}, u32[]{:S(2)}) collective-permute-start(bf16[128,2048]{1,0:T(8,128)(2,1)S(1)} %collective-permute-done.4), channel_id=1, source_target_pairs={{0,4},{4,8},{8,12},{12,16},{16,20},{20,24},{24,28},{28,0},{1,5},{5... | collective-permute-start | bytes 1572872 | tf_op jit(solution)/shard_map/ppermute | solution.py:17
  270.1 0.8 copy-start.6
  270.9 12.1 %collective-permute-start.6 = (bf16[128,2048]{1,0:T(8,128)(2,1)S(1)}, bf16[128,2048]{1,0:T(8,128)(2,1)S(1)}, u32[]{:S(2)}, u32[]{:S(2)}) collective-permute-start(bf16[128,2048]{1,0:T(8,128)(2,1)S(1)} %collective-permute-done.5), channel_id=1, source_target_pairs={{0,4},{4,8},{8,12},{12,16},{16,20},{20,24},{24,28},{28,0},{1,5},{5... | collective-permute-start | bytes 1572872 | tf_op jit(solution)/shard_map/ppermute | solution.py:17
  283.0 0.8 copy-start.8
  283.8 13.8 %collective-permute-start.7 = (bf16[128,2048]{1,0:T(8,128)(2,1)S(1)}, bf16[128,2048]{1,0:T(8,128)(2,1)}, u32[]{:S(2)}, u32[]{:S(2)}) collective-permute-start(bf16[128,2048]{1,0:T(8,128)(2,1)S(1)} %collective-permute-done.6), channel_id=1, source_target_pairs={{0,4},{4,8},{8,12},{12,16},{16,20},{20,24},{24,28},{28,0},{1,5},{5... | collective-permute-start | bytes 1572872 | tf_op jit(solution)/shard_map/ppermute | solution.py:17
  297.6 12.2 %collective-permute-start.8 = (bf16[128,2048]{1,0:T(8,128)(2,1)}, bf16[128,2048]{1,0:T(8,128)(2,1)}, u32[]{:S(2)}, u32[]{:S(2)}) collective-permute-start(bf16[128,2048]{1,0:T(8,128)(2,1)} %collective-permute-done.7), channel_id=1, source_target_pairs={{0,4},{4,8},{8,12},{12,16},{16,20},{20,24},{24,28},{28,0},{1,5},{5... | collective-permute-start | bytes 1572872 | tf_op jit(solution)/shard_map/ppermute | solution.py:17
  297.6 21.0 %copy-start.9 = (bf16[128,2048]{1,0:T(8,128)(2,1)S(1)}, bf16[128,2048]{1,0:T(8,128)(2,1)}, u32[]{:S(2)}) copy-start(bf16[128,2048]{1,0:T(8,128)(2,1)} %copy-done.8) | copy-start | bytes 1572868
  297.6 21.1 %copy-start.7 = (bf16[128,2048]{1,0:T(8,128)(2,1)S(1)}, bf16[128,2048]{1,0:T(8,128)(2,1)}, u32[]{:S(2)}) copy-start(bf16[128,2048]{1,0:T(8,128)(2,1)} %copy-done.6) | copy-start | bytes 1572868
  297.6 21.1 %copy-start.5 = (bf16[128,2048]{1,0:T(8,128)(2,1)S(1)}, bf16[128,2048]{1,0:T(8,128)(2,1)}, u32[]{:S(2)}) copy-start(bf16[128,2048]{1,0:T(8,128)(2,1)} %copy-done.4) | copy-start | bytes 1572868
  297.6 21.2 %copy-start.3 = (bf16[128,2048]{1,0:T(8,128)(2,1)S(1)}, bf16[128,2048]{1,0:T(8,128)(2,1)}, u32[]{:S(2)}) copy-start(bf16[128,2048]{1,0:T(8,128)(2,1)} %copy-done.2) | copy-start | bytes 1572868
Sparse Core Ops, SparseCore 0:
  49.7 86.9 reduce-scatter.2
  154.7 36.6 all-reduce.7
  342.6 23.5 reduce-scatter.4
